TPU v7x, 256 devices: a whole 4x4x8 slice. The times are simulated.
256 devices in a mesh: leaf: 2 (over core), row: 8 (over z), col: 16 (over y, x).
Axes of the slice: x: 4, y: 4, z: 8, core: 2. Of those that a mesh axis runs over, the one named last changes fastest.
Arguments:
- front: float32 [2, 8, 8, 128, 4, 16, 128], P('leaf', None, 'row', None, None, 'col'), as said below
- parent: float32 [4, 2, 8, 128, 4, 16, 128], P(None, 'leaf', 'row', None, None, 'col'), may hold values from -0.2 to 0.2
- tile_map: int32 [2, 56], replicated, may hold values from 0 to 63, as said below
- col_shift: int32 [4], replicated, may hold values from 0 to 7
Outputs:
- factored: float32 [2, 8, 8, 128, 4, 16, 128], P('leaf', None, 'row', None, None, 'col')
- new_parent: float32 [4, 2, 8, 128, 4, 16, 128], P(None, 'leaf', 'row', None, None, 'col')
Inputs may be any that keep to these rules, and one draw needn't show every extreme that they name: For each leaf the 8192 x 8192 matrix read from front is symmetric positive definite. Entry [l, e] names the parent tile joined by tile 8 + e of child l; no row repeats a value. The parent tile q = tile_map[l, e] has (q mod 16 + col_shift[q // 16]) mod 16 equal to (8 + e) mod 16. Among the tiles of one child whose indices are equal mod 8, at most 1 have parent tiles equal mod 16.
All inputs are finite; a program needn't handle non-finite values.
Results may differ from a plain program's by a relative error of at most 0.0001.
Values sent between devices are 32-bit elements; how exact they have to be, the bound alone decides.
No kernel may reach another device: no remote copies, remote signals or barrier semaphores. Data moves between devices by JAX's collectives and lax.ppermute only.
A program may use at most 128 MiB of HBM per device.

v0:
```python
import jax
import jax.numpy as jnp
from jax import lax
from jax.sharding import PartitionSpec as P

TILE = 128
PB = 512
PANELS = 2
NPIV = 1024
HIGHEST = lax.Precision.HIGHEST


def spread(value, axis, source):
    kept = jnp.where(lax.axis_index(axis) == source, value, 0).astype(value.dtype)
    return lax.psum(kept, axis)


def update_slots(working, next_rows, column_factor, slot_low, slot_high):
    product = jnp.einsum(
        "atp,bsp->atbs",
        next_rows,
        column_factor,
        precision=HIGHEST,
        preferred_element_type=jnp.float32,
    )
    return working.at[:, :, slot_low:slot_high, :].add(-product)


def per_device(front, parent, tile_map, col_shift):
    leaf_count = lax.axis_size("leaf")
    row_count = lax.axis_size("row")
    col_count = lax.axis_size("col")
    leaf_index = lax.axis_index("leaf")
    row_index = lax.axis_index("row")
    col_index = lax.axis_index("col")
    local_front = front[0, :, 0, :, :, 0, :]
    row_slots = local_front.shape[0]
    col_slots = local_front.shape[2]
    panel_tiles = PB // TILE
    pivot_tiles = NPIV // TILE
    row_tiles = jnp.arange(row_slots, dtype=jnp.int32) * row_count + row_index
    col_tiles = jnp.arange(col_slots, dtype=jnp.int32) * col_count + col_index

    def fetch_panel(working, panel_index):
        pieces = []
        for offset in range(panel_tiles):
            column = panel_index * panel_tiles + offset
            column_tile = working[:, :, column // col_count, :]
            pieces.append(spread(column_tile, "col", column % col_count))
        return jnp.concatenate(pieces, axis=2)

    def write_factor(working, factor, panel_index):
        first_column = panel_index * panel_tiles
        slot_values = sorted(
            set([(first_column + offset) // col_count for offset in range(panel_tiles)])
        )
        for slot_index in slot_values:
            current = working[:, :, slot_index, :]
            for offset in range(panel_tiles):
                column = first_column + offset
                if column // col_count == slot_index:
                    current = jnp.where(
                        col_index == column % col_count,
                        factor[:, :, offset * TILE : (offset + 1) * TILE],
                        current,
                    )
            working = working.at[:, :, slot_index, :].set(current)
        return working

    working = local_front
    panel_block = fetch_panel(working, 0)
    for panel_index in range(PANELS):
        first_tile = panel_index * panel_tiles
        factor_slot_index = first_tile // row_count
        start_row = first_tile % row_count
        gathered = lax.all_gather(panel_block[factor_slot_index], "row", axis=0, tiled=True)
        diagonal_block = gathered[start_row * TILE : (start_row + panel_tiles) * TILE]
        lower_factor = jnp.linalg.cholesky(diagonal_block)
        factor_flattened = panel_block.reshape(row_slots * TILE, PB)
        solved = lax.linalg.triangular_solve(
            lower_factor, factor_flattened, left_side=False, lower=True, transpose_a=True
        )
        solved = solved.reshape(row_slots, TILE, PB)
        offset_tile = jnp.clip(row_index - start_row, 0, panel_tiles - 1)
        diagonal_rows = lax.dynamic_slice_in_dim(lower_factor, offset_tile * TILE, TILE, 0)
        in_panel = (row_tiles >= first_tile) & (row_tiles < first_tile + panel_tiles)
        factor_factor = jnp.where(in_panel[:, None, None], diagonal_rows[None], solved)
        factor_factor = jnp.where((row_tiles >= first_tile)[:, None, None], factor_factor, 0.0)
        next_rows = jnp.where(
            (row_tiles >= first_tile + panel_tiles)[:, None, None], factor_factor, 0.0
        )
        group_size = col_count // row_count
        owner_rows = spread(next_rows, "row", col_index % row_count)
        grouped = owner_rows.reshape(col_slots, group_size, TILE, PB)
        column_factor = lax.dynamic_index_in_dim(grouped, col_index // row_count, 1, keepdims=False)
        column_factor = jnp.where(
            (col_tiles >= first_tile + panel_tiles)[:, None, None], column_factor, 0.0
        )
        factor, next_rows, column_factor = (factor_factor, next_rows, column_factor)
        working = update_slots(working, next_rows, column_factor, 0, col_slots)
        upcoming = (
            fetch_panel(working, panel_index + 1) if panel_index + 1 < PANELS else panel_block
        )
        working = write_factor(working, factor, panel_index)
        panel_block = upcoming
    upper_part = (row_tiles < pivot_tiles)[:, None, None, None] & (col_tiles >= pivot_tiles)[
        None, None, :, None
    ]
    working = jnp.where(upper_part, 0.0, working)
    factored = working.reshape(front.shape)
    contribution = jnp.where((col_tiles >= pivot_tiles)[None, None, :, None], working, 0.0)
    contrib_count = tile_map.shape[1]
    entry_ids = jnp.arange(contrib_count, dtype=jnp.int32)
    own_map = lax.dynamic_index_in_dim(tile_map, leaf_index, 0, keepdims=False)
    row_match = (row_tiles - pivot_tiles)[:, None] == entry_ids[None, :]
    row_targets = jnp.sum(jnp.where(row_match, own_map[None, :], 0), axis=1)
    row_valid = row_tiles >= pivot_tiles
    owner_count = leaf_count * row_count
    destination = row_targets % owner_count
    parent_row_slot = row_targets // owner_count
    slot_ids = jnp.arange(row_slots, dtype=jnp.int32)
    same_before = (
        (destination[None, :] == destination[:, None])
        & row_valid[None, :]
        & (slot_ids[None, :] < slot_ids[:, None])
    )
    rank_in_dest = jnp.sum(same_before.astype(jnp.int32), axis=1)
    capacity = (col_slots + row_count - 1) // row_count
    owner_ids = jnp.arange(owner_count, dtype=jnp.int32)
    capacity_ids = jnp.arange(capacity, dtype=jnp.int32)
    selection = (
        row_valid[None, None, :]
        & (destination[None, None, :] == owner_ids[:, None, None])
        & (rank_in_dest[None, None, :] == capacity_ids[None, :, None])
    )
    flattened = contribution.reshape(row_slots, -1)
    send_buffer = jnp.einsum(
        "oka,ax->okx",
        selection.astype(jnp.float32),
        flattened,
        precision=HIGHEST,
        preferred_element_type=jnp.float32,
    )
    chosen_slot = jnp.sum(jnp.where(selection, parent_row_slot[None, None, :], 0), axis=2)
    send_slots = jnp.where(jnp.any(selection, axis=2), chosen_slot, -1)
    received, received_slots = (
        lax.all_to_all(send_buffer, ("leaf", "row"), split_axis=0, concat_axis=0, tiled=True),
        lax.all_to_all(send_slots, ("leaf", "row"), split_axis=0, concat_axis=0, tiled=True),
    )
    received = received.reshape(leaf_count, row_count, capacity, -1)
    received_slots = received_slots.reshape(leaf_count, row_count, capacity)
    parent_local = parent[:, 0, 0, :, :, 0, :]
    parent_rows = parent_local.shape[0]
    parent_cols = parent_local.shape[2]
    row_place = (
        received_slots[None] == jnp.arange(parent_rows, dtype=jnp.int32)[:, None, None, None]
    ).astype(jnp.float32)
    by_leaf = jnp.einsum(
        "slrk,lrkx->slx", row_place, received, precision=HIGHEST, preferred_element_type=jnp.float32
    )
    by_leaf = by_leaf.reshape(parent_rows, leaf_count, TILE, col_slots, TILE)
    col_match = (col_tiles - pivot_tiles)[:, None] == entry_ids[None, :]
    col_targets = jnp.sum(jnp.where(col_match[None], tile_map[:, None, :], 0), axis=2)
    col_valid = col_tiles >= pivot_tiles
    parent_slot_ids = jnp.arange(parent_cols, dtype=jnp.int32)
    col_place = (
        col_valid[None, None, :]
        & (col_targets[:, None, :] // col_count == parent_slot_ids[None, :, None])
    ).astype(jnp.float32)
    assembled = jnp.einsum(
        "sltbv,lub->stuv", by_leaf, col_place, precision=HIGHEST, preferred_element_type=jnp.float32
    )
    new_parent = (parent_local + assembled).reshape(parent.shape)
    return (factored, new_parent)


def solution(mesh):
    return jax.shard_map(
        per_device,
        mesh=mesh,
        in_specs=(
            P("leaf", None, "row", None, None, "col", None),
            P(None, "leaf", "row", None, None, "col", None),
            P(),
            P(),
        ),
        out_specs=(
            P("leaf", None, "row", None, None, "col", None),
            P(None, "leaf", "row", None, None, "col", None),
        ),
        check_vma=False,
    )
```

profile of v0, /device:TPU:1, one launch (start us, length us, event | category | flops | bytes accessed | tf_op | source)
XLA Modules:
  0.0 995.7 jit_solution(4092188100553603286)
XLA Ops:
  7.2 4.6 copy.98
  13.8 103.2 %all-reduce.14.cloned.1.call-done = (f32[8,128,128]{1,2,0:T(8,128)}, f32[8,128,128]{1,2,0:T(8,128)}, f32[8,128,128]{1,2,0:T(8,128)}, f32[8,128,128]{1,2,0:T(8,128)}) async-done(((f32[8,128,128]{1,2,0:T(8,128)}, f32[8,128,128]{1,2,0:T(8,128)}, f32[8,128,128]{1,2,0:T(8,128)}, f32[8,128,128]{1,2,0:T(8,128)}), (f32[8,128,128]{1,2,0:T(8,128)}, f32[8,128,128]{1,2,0:T(8,128)}, f32[8,128,128]{1,2,0:T(8,128)}, ...) | async-done | bytes 2097168 | tf_op jit(solution)/shard_map/psum | solution.py:15
  124.1 41.6 %all-gather.5.cloned.1.call-done = f32[1,1024,512]{1,2,0:T(8,128)} async-done(((f32[1,128,512]{1,2,0:T(8,128)}), f32[1,1024,512]{1,2,0:T(8,128)}) %all-gather.5.cloned.1.call-update) | async-done | bytes 2097168 | tf_op jit(solution)/shard_map/all_gather | solution.py:76
  165.7 2.3 slice_bitcast_fusion.1
  172.0 11.7 %cholesky.286 = f32[128,128]{1,0:T(8,128)S(1)} custom-call(f32[128,128]{1,0:T(8,128)S(1)} %cholesky.426), custom_call_target="Cholesky" | custom-call | tf_op jit(solution)/shard_map/jit(cholesky)/cholesky | solution.py:78
  183.8 9.8 custom-call.27
  196.2 11.7 %cholesky.305 = f32[128,128]{1,0:T(8,128)S(1)} custom-call(f32[128,128]{1,0:T(8,128)S(1)} %cholesky.430), custom_call_target="Cholesky" | custom-call | tf_op jit(solution)/shard_map/jit(cholesky)/cholesky | solution.py:78
  207.9 10.0 custom-call.28
  219.5 11.7 %cholesky.326 = f32[128,128]{1,0:T(8,128)S(1)} custom-call(f32[128,128]{1,0:T(8,128)S(1)} %cholesky.435), custom_call_target="Cholesky" | custom-call | tf_op jit(solution)/shard_map/jit(cholesky)/cholesky | solution.py:78
  231.2 9.8 custom-call.29
  242.5 11.7 %cholesky.343 = f32[128,128]{1,0:T(8,128)S(1)} custom-call(f32[128,128]{1,0:T(8,128)S(1)} %convolution_subtract_fusion.9), custom_call_target="Cholesky" | custom-call | tf_op jit(solution)/shard_map/jit(cholesky)/cholesky | solution.py:78
  260.8 11.7 %while.10 = (s32[]{:T(128)}, f32[512,512]{1,0:T(8,128)}, s32[4,2]{0,1:T(2,128)S(1)}, f32[4,128,128]{2,1,0:T(8,128)S(1)}, s32[]{:T(128)}) while((s32[]{:T(128)}, f32[512,512]{1,0:T(8,128)}, s32[4,2]{0,1:T(2,128)S(1)}, f32[4,128,128]{2,1,0:T(8,128)S(1)}, s32[]{:T(128)}) %tuple.99), condition=%wide.while_cond.4, body=%wide.while_body.4.sunk | while | flops 2 | bytes 131189 | solution.py:80
  261.4 2.2 bitcast_dynamic-update-slice_fusion.4
  264.4 2.2 bitcast_dynamic-update-slice_fusion.4
  267.3 2.2 bitcast_dynamic-update-slice_fusion.4
  270.3 2.2 bitcast_dynamic-update-slice_fusion.4
  272.5 39.3 %custom-call.30 = f32[4,128,128]{1,2,0:T(8,128)S(1)} custom-call(f32[4,128,128]{2,1,0:T(8,128)S(1)} %get-tuple-element.82), custom_call_target="InvertDiagBlocksLowerTriangular" | custom-call | tf_op jit(solution)/shard_map/triangular_solve/custom-call.3 | solution.py:80
  314.9 2.7 convolution_subtract_fusion.1
  318.3 3.8 fusion.18
  327.4 3.9 pad_maximum_fusion
  331.2 2.9 copy.104
  334.2 2.9 copy.105
  337.1 4.0 select_select_fusion.3
  341.1 2.9 copy.106
  346.0 79.9 %all-reduce.8.cloned.1.call-done = f32[4,2,128,512]{3,2,0,1:T(8,128)} async-done(((f32[4,2,128,512]{3,2,0,1:T(8,128)}), f32[4,2,128,512]{3,2,0,1:T(8,128)}) %all-reduce.8.cloned.1.call-update) | async-done | bytes 2097168 | tf_op jit(solution)/shard_map/psum | solution.py:15
  425.9 5.8 negate_add_fusion.1
  433.2 101.6 %all-reduce.12.cloned.1.call-done = (f32[8,128,128]{1,2,0:T(8,128)}, f32[8,128,128]{1,2,0:T(8,128)}, f32[8,128,128]{1,2,0:T(8,128)}, f32[8,128,128]{1,2,0:T(8,128)}) async-done(((f32[8,128,128]{1,2,0:T(8,128)}, f32[8,128,128]{1,2,0:T(8,128)}, f32[8,128,128]{1,2,0:T(8,128)}, f32[8,128,128]{1,2,0:T(8,128)}), (f32[8,128,128]{1,2,0:T(8,128)}, f32[8,128,128]{1,2,0:T(8,128)}, f32[8,128,128]{1,2,0:T(8,128)}, ...) | async-done | bytes 2097168 | tf_op jit(solution)/shard_map/psum | solution.py:15
  539.3 3.0 copy.112
  542.4 41.1 %all-gather.7.cloned.1.call-done = f32[1,1024,512]{1,2,0:T(8,128)} async-done(((f32[1,128,512]{1,2,0:T(8,128)}), f32[1,1024,512]{1,2,0:T(8,128)}) %all-gather.7.cloned.1.call-update) | async-done | bytes 2097168 | tf_op jit(solution)/shard_map/all_gather | solution.py:76
  583.5 2.3 slice_bitcast_fusion
  589.7 11.7 %cholesky.358 = f32[128,128]{1,0:T(8,128)S(1)} custom-call(f32[128,128]{1,0:T(8,128)S(1)} %cholesky.439), custom_call_target="Cholesky" | custom-call | tf_op jit(solution)/shard_map/jit(cholesky)/cholesky | solution.py:78
  601.6 9.8 custom-call.31
  614.0 11.7 %cholesky.377 = f32[128,128]{1,0:T(8,128)S(1)} custom-call(f32[128,128]{1,0:T(8,128)S(1)} %cholesky.443), custom_call_target="Cholesky" | custom-call | tf_op jit(solution)/shard_map/jit(cholesky)/cholesky | solution.py:78
  625.7 10.0 %custom-call.32 = f32[1,128,128]{1,2,0:T(8,128)S(1)} custom-call(f32[1,128,128]{2,1,0:T(8,128)S(1)} %get-tuple-element.150), custom_call_target="InvertDiagBlocksLowerTriangular" | custom-call | tf_op jit(solution)/shard_map/jit(cholesky)/cholesky | solution.py:78
  637.3 11.7 %cholesky.398 = f32[128,128]{1,0:T(8,128)S(1)} custom-call(f32[128,128]{1,0:T(8,128)S(1)} %cholesky.448), custom_call_target="Cholesky" | custom-call | tf_op jit(solution)/shard_map/jit(cholesky)/cholesky | solution.py:78
  649.0 9.8 custom-call.33
  660.3 11.7 %cholesky.415 = f32[128,128]{1,0:T(8,128)S(1)} custom-call(f32[128,128]{1,0:T(8,128)S(1)} %convolution_subtract_fusion.8), custom_call_target="Cholesky" | custom-call | tf_op jit(solution)/shard_map/jit(cholesky)/cholesky | solution.py:78
  679.1 11.4 %while.11 = (s32[]{:T(128)}, f32[512,512]{1,0:T(8,128)}, s32[4,2]{0,1:T(2,128)S(1)}, f32[4,128,128]{2,1,0:T(8,128)S(1)}, s32[]{:T(128)}) while((s32[]{:T(128)}, f32[512,512]{1,0:T(8,128)}, s32[4,2]{0,1:T(2,128)S(1)}, f32[4,128,128]{2,1,0:T(8,128)S(1)}, s32[]{:T(128)}) %tuple.119), condition=%wide.while_cond.4.clone, body=%wide.while_body.4.clone.sunk | while | flops 2 | bytes 131189 | solution.py:80
  679.7 2.2 bitcast_dynamic-update-slice_fusion.5
  682.6 2.2 bitcast_dynamic-update-slice_fusion.5
  685.4 2.2 bitcast_dynamic-update-slice_fusion.5
  690.5 39.3 %custom-call.34 = f32[4,128,128]{1,2,0:T(8,128)S(1)} custom-call(f32[4,128,128]{2,1,0:T(8,128)S(1)} %get-tuple-element.83), custom_call_target="InvertDiagBlocksLowerTriangular" | custom-call | tf_op jit(solution)/shard_map/triangular_solve/custom-call.3 | solution.py:80
  734.4 2.7 convolution_subtract_fusion
  737.7 3.8 fusion.15
  746.3 3.0 copy.113
  749.3 4.8 pad_maximum_fusion.1
  754.1 2.9 copy.114
  757.0 3.1 copy.115
  760.1 4.0 select_select_fusion
  764.1 2.9 copy.116
  767.9 9.3 all-to-all-start.1
  779.0 2.9 copy.132
  781.9 67.1 %all-reduce.10.cloned.1.call-done = f32[4,2,128,512]{3,2,0,1:T(8,128)} async-done(((f32[4,2,128,512]{3,2,0,1:T(8,128)}), f32[4,2,128,512]{3,2,0,1:T(8,128)}) %all-reduce.10.cloned.1.call-update) | async-done | bytes 2097168 | tf_op jit(solution)/shard_map/psum | solution.py:15
  849.1 5.6 negate_add_fusion
  856.8 3.1 copy.119
  859.9 3.9 reshape.731
  863.8 3.5 convolution_bitcast_fusion
  867.3 6.3 copy.120
  873.6 8.6 all-to-all-start
  882.9 3.6 copy.123
  886.5 88.3 %all-to-all-done = f32[16,1,65536]{2,1,0:T(1,128)} async-done(((f32[16,1,65536]{2,1,0:T(1,128)}), f32[16,1,65536]{2,1,0:T(1,128)}, u32[]{:S(2)}, u32[]{:S(2)}) %all-to-all-start) | async-done | bytes 4194336 | tf_op jit(solution)/shard_map/all_to_all | solution.py:147
  974.8 7.8 convolution_bitcast_fusion.1
  982.6 3.1 reshape.733
  985.8 2.8 fusion.14
  (171 shorter events, 75.7 us)
Async XLA Ops:
  7.2 109.8 %all-reduce.14.cloned.1.call-start = ((), (), s32[]{:S(2)}) async-start(), calls=%async_computation.7 | async-start | bytes 4194304 | tf_op jit(solution)/shard_map/psum | solution.py:15
  11.8 2.0 copy-start
  13.8 151.9 %all-gather.5.cloned.1.call-start = ((), (), s32[]{:S(2)}) async-start(), calls=%async_computation.4 | async-start | bytes 2359296 | tf_op jit(solution)/shard_map/all_gather | solution.py:76
  117.0 2.3 copy-start.14
  117.0 2.3 copy-start.12
  118.1 3.4 copy-start.16
  119.3 1.3 copy-start.5
  121.4 304.5 %all-reduce.8.cloned.1.call-start = ((), (), s32[]{:S(2)}) async-start(), calls=%async_computation.2 | async-start | bytes 4194304 | tf_op jit(solution)/shard_map/psum | solution.py:15
  171.0 1.0 copy-start.7
  318.3 3.8 copy-start.4
  334.2 2.9 copy-start.11
  344.1 190.7 %all-reduce.12.cloned.1.call-start = ((), (), s32[]{:S(2)}) async-start(), calls=%async_computation.6 | async-start | bytes 4194304 | tf_op jit(solution)/shard_map/psum | solution.py:15
  433.1 150.4 %all-gather.7.cloned.1.call-start = ((), (), s32[]{:S(2)}) async-start(), calls=%async_computation.5 | async-start | bytes 2359296 | tf_op jit(solution)/shard_map/all_gather | solution.py:76
  534.8 2.3 copy-start.15
  534.8 2.3 copy-start.13
  537.1 1.3 copy-start.6
  539.2 309.9 %all-reduce.10.cloned.1.call-start = ((), (), s32[]{:S(2)}) async-start(), calls=%async_computation.3 | async-start | bytes 4194304 | tf_op jit(solution)/shard_map/psum | solution.py:15
  588.8 1.0 copy-start.8
  729.8 4.6 copy-start.1
  737.7 3.8 copy-start.3
  757.0 3.1 copy-start.10
  767.9 105.7 %all-to-all-start.1 = ((s32[16,1,1]{2,1,0:T(1,128)}), s32[16,1,1]{2,1,0:T(1,128)S(1)}, u32[]{:S(2)}, u32[]{:S(2)}) async-start(s32[16,1,1]{2,1,0:T(1,128)} %copy.121), calls=%async_computation.1 | async-start | bytes 16384 | tf_op jit(solution)/shard_map/all_to_all | solution.py:148
  849.1 5.7 copy-start.2
  873.6 101.2 %all-to-all-start = ((f32[16,1,65536]{2,1,0:T(1,128)}), f32[16,1,65536]{2,1,0:T(1,128)}, u32[]{:S(2)}, u32[]{:S(2)}) async-start(f32[16,1,65536]{2,1,0:T(1,128)} %copy.120), calls=%async_computation | async-start | bytes 8388608 | tf_op jit(solution)/shard_map/all_to_all | solution.py:147
  982.6 3.1 copy-start.9
Sparse Core Ops, SparseCore 0:
  13.5 103.4 all-reduce.13
  121.5 44.1 all-gather.4
  344.2 81.6 all-reduce.7
  433.2 101.4 all-reduce.11
  539.3 44.1 all-gather.6
  767.2 81.8 all-reduce.9
where the time goes:
time: 1010 us; the launch traced here: 996 us
  waiting for transfers between devices  523 us (52%)
  other arithmetic  267 us (26%)
  local copies, waits for them, and re-layouts  105 us (10%)
  matrix products  61.2 us (6%)
  between operations  21 us (2%)
  starting transfers between devices  18.2 us (2%)
    psum x4, waiting for transfers between devices, spread(): return lax.psum(kept, axis)  352 us
    another operation x29, other arithmetic, per_device(): lower_factor = jnp.linalg.cholesky(diagonal_block)  158 us
    another operation x7, other arithmetic, per_device(): lax.linalg.triangular_solve(lower_factor, factor_flattened, left_side=Fal...  90.5 us
    all_to_all x1, waiting for transfers between devices, per_device(): lax.all_to_all(send_buffer, ('leaf', 'row'), split_axis=0, concat_axis=0,...  88.3 us
    all_gather x2, waiting for transfers between devices, per_device(): lax.all_gather(panel_block[factor_slot_index], 'row', axis=0, tiled=True)  82.7 us
    another operation x29, local copies, waits for them, and re-layouts, per_device(): lax.linalg.triangular_solve(lower_factor, factor_flattened, left_side=Fal...  28.8 us
    another operation x14, matrix products, per_device(): lax.linalg.triangular_solve(lower_factor, factor_flattened, left_side=Fal...  24.7 us
  transfers between devices with their start and end apart: 8, of which 7 were waited for; matrix products, arithmetic and copies ran while one was open for 4% of the time, Pallas kernels for 0%

commit v1 on v0

--- a/solution.py
+++ b/solution.py
@@ -12,7 +12,7 @@
 
 def spread(value, axis, source):
     kept = jnp.where(lax.axis_index(axis) == source, value, 0).astype(value.dtype)
-    return lax.psum(kept, axis)
+    return jnp.sum(lax.all_gather(kept, axis), axis=0)
 
 
 def update_slots(working, next_rows, column_factor, slot_low, slot_high):

time: 1010 us -> 1610 us (1.59)
  waiting for transfers between devices: 523 us -> 1090 us
  other arithmetic: 267 us -> 323 us
    all_gather x0 -> x10, waiting for transfers between devices: none -> 920 us  [spread(): return jnp.sum(lax.all_gather(kept, axis), axis=0)]
    psum x4 -> x0, waiting for transfers between devices: 352 us -> none  [spread(): return lax.psum(kept, axis)]
    reduce_sum x0 -> x10, other arithmetic: none -> 50.3 us  [spread(): return jnp.sum(lax.all_gather(kept, axis), axis=0)]
  transfers between devices with their start and end apart: 8 -> 14, of which waited for: 7 -> 13; matrix products, arithmetic and copies ran while one was open for 4% -> 5% of each run, Pallas kernels for 0% -> 0%
where the time goes in v1:
time: 1610 us
  waiting for transfers between devices  1090 us (68%)
  other arithmetic  323 us (20%)
  local copies, waits for them, and re-layouts  93.7 us (6%)
  matrix products  60.5 us (4%)
  between operations  20.4 us (1%)
    all_gather x10, waiting for transfers between devices, spread(): return jnp.sum(lax.all_gather(kept, axis), axis=0)  920 us
    another operation x29, other arithmetic, per_device(): lower_factor = jnp.linalg.cholesky(diagonal_block)  163 us
    another operation x7, other arithmetic, per_device(): lax.linalg.triangular_solve(lower_factor, factor_flattened, left_side=Fal...  92.3 us
    all_to_all x1, waiting for transfers between devices, per_device(): lax.all_to_all(send_buffer, ('leaf', 'row'), split_axis=0, concat_axis=0,...  88.8 us
    all_gather x2, waiting for transfers between devices, per_device(): lax.all_gather(panel_block[factor_slot_index], 'row', axis=0, tiled=True)  80.1 us
    reduce_sum x10, other arithmetic, spread(): return jnp.sum(lax.all_gather(kept, axis), axis=0)  50.3 us
  transfers between devices with their start and end apart: 14, of which 13 were waited for; matrix products, arithmetic and copies ran while one was open for 5% of the time, Pallas kernels for 0%

profile of v1, /device:TPU:1, one launch (start us, length us, event | category | flops | bytes accessed | tf_op | source)
XLA Modules:
  0.0 1605.9 jit_solution(3426111488192161922)
XLA Ops:
  12.6 78.0 %all-gather.27.cloned.1.call-done = f32[128,128,1,128]{3,1,2,0:T(8,128)} async-done(((f32[8,128,1,128]{3,1,2,0:T(8,128)}), f32[128,128,1,128]{3,1,2,0:T(8,128)}) %all-gather.27.cloned.1.call-update) | async-done | bytes 8388624 | tf_op jit(solution)/shard_map/all_gather | solution.py:15
  90.6 3.9 reduce_sum.126
  94.7 74.4 %all-gather.29.cloned.1.call-done = f32[128,128,1,128]{3,1,2,0:T(8,128)} async-done(((f32[8,128,1,128]{3,1,2,0:T(8,128)}), f32[128,128,1,128]{3,1,2,0:T(8,128)}) %all-gather.29.cloned.1.call-update) | async-done | bytes 8388624 | tf_op jit(solution)/shard_map/all_gather | solution.py:15
  169.1 3.9 reduce_sum.127
  173.3 73.8 %all-gather.31.cloned.1.call-done = f32[128,128,1,128]{3,1,2,0:T(8,128)} async-done(((f32[8,128,1,128]{3,1,2,0:T(8,128)}), f32[128,128,1,128]{3,1,2,0:T(8,128)}) %all-gather.31.cloned.1.call-update) | async-done | bytes 8388624 | tf_op jit(solution)/shard_map/all_gather | solution.py:15
  247.1 3.9 reduce_sum.128
  252.0 72.9 %all-gather.33.cloned.1.call-done = f32[128,128,1,128]{3,1,2,0:T(8,128)} async-done(((f32[8,128,1,128]{3,1,2,0:T(8,128)}), f32[128,128,1,128]{3,1,2,0:T(8,128)}) %all-gather.33.cloned.1.call-update) | async-done | bytes 8388624 | tf_op jit(solution)/shard_map/all_gather | solution.py:15
  324.9 3.9 reduce_sum.129
  334.3 41.1 %all-gather.35.cloned.1.call-done = f32[1,1024,512]{1,2,0:T(8,128)} async-done(((f32[1,128,512]{1,2,0:T(8,128)}), f32[1,1024,512]{1,2,0:T(8,128)}) %all-gather.35.cloned.1.call-update) | async-done | bytes 2097168 | tf_op jit(solution)/shard_map/all_gather | solution.py:76
  378.5 11.7 cholesky.286
  390.2 9.8 custom-call.27
  400.9 11.7 cholesky.305
  412.6 10.0 custom-call.28
  423.3 11.7 cholesky.326
  435.7 9.8 custom-call.29
  446.2 11.7 cholesky.343
  461.9 3.4 fusion.32
  465.3 11.7 while.10
  477.0 39.3 %custom-call.30 = f32[4,128,128]{1,2,0:T(8,128)S(1)} custom-call(f32[4,128,128]{2,1,0:T(8,128)S(1)} %get-tuple-element.82), custom_call_target="InvertDiagBlocksLowerTriangular" | custom-call | tf_op jit(solution)/shard_map/triangular_solve/custom-call.3 | solution.py:80
  519.5 2.7 convolution_subtract_fusion.1
  522.9 3.8 fusion.18
  532.6 3.8 pad_maximum_fusion.1
  540.5 2.9 copy.179
  543.4 172.7 %all-gather.23.cloned.1.call-done = f32[8,8,128,512]{3,2,1,0:T(8,128)} async-done(((f32[1,8,128,512]{3,2,1,0:T(8,128)}), f32[8,8,128,512]{3,2,1,0:T(8,128)}) %all-gather.23.cloned.1.call-update) | async-done | bytes 16777232 | tf_op jit(solution)/shard_map/all_gather | solution.py:15
  716.0 9.4 reduce_sum.130
  725.5 6.1 bitcast_add_fusion
  736.4 72.4 %all-gather.37.cloned.1.call-done = f32[128,128,1,128]{3,1,2,0:T(8,128)} async-done(((f32[8,128,1,128]{3,1,2,0:T(8,128)}), f32[128,128,1,128]{3,1,2,0:T(8,128)}) %all-gather.37.cloned.1.call-update) | async-done | bytes 8388624 | tf_op jit(solution)/shard_map/all_gather | solution.py:15
  808.8 3.9 reduce_sum.131
  813.0 73.8 %all-gather.43.cloned.1.call-done = f32[128,128,1,128]{3,1,2,0:T(8,128)} async-done(((f32[8,128,1,128]{3,1,2,0:T(8,128)}), f32[128,128,1,128]{3,1,2,0:T(8,128)}) %all-gather.43.cloned.1.call-update) | async-done | bytes 8388624 | tf_op jit(solution)/shard_map/all_gather | solution.py:15
  886.8 3.9 reduce_sum.134
  891.7 73.0 %all-gather.41.cloned.1.call-done = f32[128,128,1,128]{3,1,2,0:T(8,128)} async-done(((f32[8,128,1,128]{3,1,2,0:T(8,128)}), f32[128,128,1,128]{3,1,2,0:T(8,128)}) %all-gather.41.cloned.1.call-update) | async-done | bytes 8388624 | tf_op jit(solution)/shard_map/all_gather | solution.py:15
  964.8 3.9 reduce_sum.133
  969.8 72.8 %all-gather.39.cloned.1.call-done = f32[128,128,1,128]{3,1,2,0:T(8,128)} async-done(((f32[8,128,1,128]{3,1,2,0:T(8,128)}), f32[128,128,1,128]{3,1,2,0:T(8,128)}) %all-gather.39.cloned.1.call-update) | async-done | bytes 8388624 | tf_op jit(solution)/shard_map/all_gather | solution.py:15
  1042.6 3.9 reduce_sum.132
  1052.4 3.1 copy.160
  1055.6 39.0 %all-gather.45.cloned.1.call-done = f32[1,1024,512]{1,2,0:T(8,128)} async-done(((f32[1,128,512]{1,2,0:T(8,128)}), f32[1,1024,512]{1,2,0:T(8,128)}) %all-gather.45.cloned.1.call-update) | async-done | bytes 2097168 | tf_op jit(solution)/shard_map/all_gather | solution.py:76
  1100.8 11.7 cholesky.358
  1113.2 9.8 custom-call.31
  1126.4 11.7 cholesky.377
  1138.8 10.2 custom-call.32
  1152.1 13.2 cholesky.398
  1167.4 11.3 custom-call.33
  1181.0 11.7 cholesky.415
  1197.7 11.1 while.11
  1208.8 39.3 %custom-call.34 = f32[4,128,128]{1,2,0:T(8,128)S(1)} custom-call(f32[4,128,128]{2,1,0:T(8,128)S(1)} %get-tuple-element.83), custom_call_target="InvertDiagBlocksLowerTriangular" | custom-call | tf_op jit(solution)/shard_map/triangular_solve/custom-call.3 | solution.py:80
  1257.0 3.8 fusion.15
  1264.7 2.9 copy.182
  1267.7 4.8 pad_maximum_fusion.3
  1272.5 2.9 copy.184
  1275.5 3.4 select_select_fusion.1
  1280.8 9.3 all-to-all-start.1
  1293.4 3.6 copy.183
  1298.8 156.0 %all-gather.25.cloned.1.call-done = f32[8,8,128,512]{3,2,1,0:T(8,128)} async-done(((f32[1,8,128,512]{3,2,1,0:T(8,128)}), f32[8,8,128,512]{3,2,1,0:T(8,128)}) %all-gather.25.cloned.1.call-update) | async-done | bytes 16777232 | tf_op jit(solution)/shard_map/all_gather | solution.py:15
  1454.8 9.4 reduce_sum.135
  1464.1 5.6 negate_add_fusion
  1473.2 3.9 reshape.867
  1477.1 3.5 convolution_bitcast_fusion
  1480.6 6.5 copy.168
  1487.1 5.0 all-to-all-start
  1492.8 3.5 copy.171
  1496.3 88.8 %all-to-all-done = f32[16,1,65536]{2,1,0:T(1,128)} async-done(((f32[16,1,65536]{2,1,0:T(1,128)}), f32[16,1,65536]{2,1,0:T(1,128)}, u32[]{:S(2)}, u32[]{:S(2)}) %all-to-all-start) | async-done | bytes 4194336 | tf_op jit(solution)/shard_map/all_to_all | solution.py:147
  1585.1 7.8 convolution_bitcast_fusion.1
  1592.9 3.1 reshape.869
  1596.0 2.8 fusion.14
  (221 shorter events, 113.1 us)
Async XLA Ops:
  7.2 83.4 %all-gather.27.cloned.1.call-start = ((), (), s32[]{:S(2)}) async-start(), calls=%async_computation.4 | async-start | bytes 8912896 | tf_op jit(solution)/shard_map/all_gather | solution.py:15
  10.5 158.7 %all-gather.29.cloned.1.call-start = ((), (), s32[]{:S(2)}) async-start(), calls=%async_computation.5 | async-start | bytes 8912896 | tf_op jit(solution)/shard_map/all_gather | solution.py:15
  11.2 235.9 %all-gather.31.cloned.1.call-start = ((), (), s32[]{:S(2)}) async-start(), calls=%async_computation.6 | async-start | bytes 8912896 | tf_op jit(solution)/shard_map/all_gather | solution.py:15
  11.9 313.0 %all-gather.33.cloned.1.call-start = ((), (), s32[]{:S(2)}) async-start(), calls=%async_computation.7 | async-start | bytes 8912896 | tf_op jit(solution)/shard_map/all_gather | solution.py:15
  12.5 362.9 %all-gather.35.cloned.1.call-start = ((), (), s32[]{:S(2)}) async-start(), calls=%async_computation.8 | async-start | bytes 2359296 | tf_op jit(solution)/shard_map/all_gather | solution.py:76
  332.0 384.1 %all-gather.23.cloned.1.call-start = ((), (), s32[]{:S(2)}) async-start(), calls=%async_computation.2 | async-start | bytes 18874368 | tf_op jit(solution)/shard_map/all_gather | solution.py:15
  332.1 206.3 %copy-start.19 = (pred[8]{0:T(512)(128)(4,1)}, pred[8]{0:T(512)(128)(4,1)S(1)}, u32[]{:S(2)}) copy-start(pred[8]{0:T(512)(128)(4,1)S(1)} %get-tuple-element.158) | copy-start | bytes 28
  332.1 206.3 %copy-start.21 = (pred[8]{0:T(512)(128)(4,1)}, pred[8]{0:T(512)(128)(4,1)S(1)}, u32[]{:S(2)}) copy-start(pred[8]{0:T(512)(128)(4,1)S(1)} %get-tuple-element.159) | copy-start | bytes 28
  457.9 4.0 copy-start.9
  461.9 54.5 %copy-start.7 = (f32[8,128,512]{2,1,0:T(8,128)S(1)}, f32[8,128,512]{2,1,0:T(8,128)}, u32[]{:S(2)}) copy-start(f32[8,128,512]{2,1,0:T(8,128)} %copy.141) | copy-start | bytes 6291460
  522.8 6.2 copy-start.11
  540.2 268.6 %all-gather.37.cloned.1.call-start = ((), (), s32[]{:S(2)}) async-start(), calls=%async_computation.9 | async-start | bytes 8912896 | tf_op jit(solution)/shard_map/all_gather | solution.py:15
  731.6 1.3 copy-start.1
  734.3 152.5 %all-gather.43.cloned.1.call-start = ((), (), s32[]{:S(2)}) async-start(), calls=%async_computation.12 | async-start | bytes 8912896 | tf_op jit(solution)/shard_map/all_gather | solution.py:15
  735.0 229.7 %all-gather.41.cloned.1.call-start = ((), (), s32[]{:S(2)}) async-start(), calls=%async_computation.11 | async-start | bytes 8912896 | tf_op jit(solution)/shard_map/all_gather | solution.py:15
  735.8 306.8 %all-gather.39.cloned.1.call-start = ((), (), s32[]{:S(2)}) async-start(), calls=%async_computation.10 | async-start | bytes 8912896 | tf_op jit(solution)/shard_map/all_gather | solution.py:15
  736.3 358.2 %all-gather.45.cloned.1.call-start = ((), (), s32[]{:S(2)}) async-start(), calls=%async_computation.13 | async-start | bytes 2359296 | tf_op jit(solution)/shard_map/all_gather | solution.py:76
  1049.0 1.3 copy-start.5
  1051.1 403.7 %all-gather.25.cloned.1.call-start = ((), (), s32[]{:S(2)}) async-start(), calls=%async_computation.3 | async-start | bytes 18874368 | tf_op jit(solution)/shard_map/all_gather | solution.py:15
  1051.2 4.4 copy-start.23
  1099.8 1.0 copy-start.14
  1125.7 0.7 copy-start.16
  1248.1 1.9 copy-start.17
  1248.1 5.5 copy-start.8
  1252.0 4.3 copy-start.18
  1257.0 6.2 copy-start.10
  1263.2 1.6 copy-start.12
  1264.7 3.0 copy-start.25
  1264.7 3.0 copy-start.26
  1272.5 2.9 copy-start.13
  1272.5 2.9 copy-start.24
  1278.9 0.7 copy-start.27
  1278.9 11.4 copy-start.20
  1278.9 11.4 copy-start.22
  1280.8 206.2 %all-to-all-start.1 = ((s32[16,1,1]{2,1,0:T(1,128)}), s32[16,1,1]{2,1,0:T(1,128)S(1)}, u32[]{:S(2)}, u32[]{:S(2)}) async-start(s32[16,1,1]{2,1,0:T(1,128)} %copy.169), calls=%async_computation.1 | async-start | bytes 16384 | tf_op jit(solution)/shard_map/all_to_all | solution.py:148
  1290.3 1.6 copy-start.2
  1290.3 1.7 slice-start
  1292.1 1.3 copy-start.3
  1293.4 3.6 copy-start
  1298.8 165.3 %copy-start.4 = (f32[8,128,4,128]{3,1,2,0:T(8,128)S(1)}, f32[8,128,4,128]{3,1,2,0:T(8,128)}, u32[]{:S(2)}) copy-start(f32[8,128,4,128]{3,1,2,0:T(8,128)} %copy-done.3) | copy-start | bytes 6291460
  1464.1 5.7 copy-start.6
  1487.1 98.0 %all-to-all-start = ((f32[16,1,65536]{2,1,0:T(1,128)}), f32[16,1,65536]{2,1,0:T(1,128)}, u32[]{:S(2)}, u32[]{:S(2)}) async-start(f32[16,1,65536]{2,1,0:T(1,128)} %copy.168), calls=%async_computation | async-start | bytes 8388608 | tf_op jit(solution)/shard_map/all_to_all | solution.py:147
  1592.9 3.1 copy-start.15
Sparse Core Ops, SparseCore 0:
  11.0 79.5 all-gather.26
  93.6 75.4 all-gather.28
  171.6 75.4 all-gather.30
  249.4 75.4 all-gather.32
  332.1 43.2 all-gather.34
  540.3 175.6 all-gather.22
  734.4 74.3 all-gather.36
  811.3 75.4 all-gather.42
  889.2 75.4 all-gather.40
  967.0 75.4 all-gather.38
  1051.2 43.2 all-gather.44
  1279.0 175.6 all-gather.24
